TPU v7x, 128 devices: a whole 4x4x4 slice. The times are simulated.
128 devices in a mesh: dp: 4 (over x), expert: 32 (over y, z, core).
Axes of the slice: x: 4, y: 4, z: 4, core: 2. Of those that a mesh axis runs over, the one named last changes fastest.
Arguments:
- tokens: bfloat16 [16384, 4096], P(('dp', 'expert')), may hold values from -6 to 6
- cotangent: bfloat16 [16384, 4096], P(('dp', 'expert')), may hold values from -6 to 6
- routes: int32 [16384], P(('dp', 'expert')), may hold values from 0 to 31, as said below
- combine: float32 [16384], P(('dp', 'expert')), may hold values from 0.05 to 1
- expert_weights: bfloat16 [32, 3, 1536, 4096], P('expert', None, 'dp'), may hold values from -0.09375 to 0.09375
Outputs:
- combined: bfloat16 [16384, 4096], P(('dp', 'expert'))
- token_grad: bfloat16 [16384, 4096], P(('dp', 'expert'))
- combine_grad: float32 [16384], P(('dp', 'expert'))
Inputs may be any that keep to these rules, and one draw needn't show every extreme that they name: `routes`: among the 128 rows of every device, two experts, the same two on every device, are each named by exactly 8 rows, and every other expert by 3 or 4 rows.
All inputs are finite; a program needn't handle non-finite values.
Results may differ from a plain program's by a relative error of at most 0.015.
Values may be sent and summed in bfloat16 or wider, within the bound.
No kernel may reach another device: no remote copies, remote signals or barrier semaphores. Data moves between devices by JAX's collectives and lax.ppermute only.
A program may use at most 192 MiB of HBM per device.

v0:
```python
import jax
import jax.numpy as jnp
from jax import lax
from jax.sharding import PartitionSpec as P


def placement(member, slot_count):
    within = jnp.sum((jnp.cumsum(member, 0) - 1) * member, 1)
    owner_group = jnp.sum(member * lax.iota(jnp.int32, member.shape[1])[None, :], 1)
    is_used = jnp.sum(member, 1) > 0
    target = owner_group * slot_count + within
    buffer_cells = lax.iota(jnp.int32, member.shape[1] * slot_count)
    return ((buffer_cells[:, None] == target[None, :]) & is_used[None, :]).astype(jnp.bfloat16)


def spread(layout, row_block):
    return jnp.dot(layout, row_block, preferred_element_type=jnp.float32).astype(jnp.bfloat16)


def collect(layout, buffer_rows):
    return lax.dot_general(
        layout, buffer_rows, (((0,), (0,)), ((), ())), preferred_element_type=jnp.float32
    )


def group_rows(values):
    return lax.all_gather(values, "dp", axis=0, tiled=True)


def group_sum(values):
    return lax.psum_scatter(values.astype(jnp.bfloat16), "dp", scatter_dimension=0, tiled=True)


def exchange(rows, experts, model_width):
    return lax.all_to_all(
        rows.reshape(experts, -1, model_width), "expert", split_axis=0, concat_axis=0, tiled=True
    ).reshape(-1, model_width)


def forward_rows(row_block, matrices):
    gate_up = jnp.einsum("rd,kfd->krf", row_block, matrices[:2], preferred_element_type=jnp.float32)
    gate_act = gate_up[0]
    up_act = gate_up[1]
    hidden = (gate_act * jax.nn.sigmoid(gate_act) * up_act).astype(jnp.bfloat16)
    partial_out = jnp.dot(hidden, matrices[2], preferred_element_type=jnp.float32)
    return (gate_act, up_act, partial_out)


def backward_rows(row_block, gate_act, up_act, matrices):
    hidden_grad = lax.dot_general(
        row_block, matrices[2], (((1,), (1,)), ((), ())), preferred_element_type=jnp.float32
    )
    squashed = jax.nn.sigmoid(gate_act)
    gate_grad = (hidden_grad * up_act * squashed * (1.0 + gate_act * (1.0 - squashed))).astype(
        jnp.bfloat16
    )
    up_grad = (hidden_grad * gate_act * squashed).astype(jnp.bfloat16)
    both_grads = jnp.stack([gate_grad, up_grad])
    return jnp.einsum("krf,kfd->rd", both_grads, matrices[:2], preferred_element_type=jnp.float32)


def shards(tokens, cotangent, routes, combine, expert_weights):
    weights = expert_weights[0]
    tok_dev = tokens.shape[0]
    model_width = tokens.shape[1]
    experts = lax.axis_size("expert")
    capacity = 2 * tok_dev // experts
    chunks = 2
    chunk_slots = capacity // chunks
    labels = lax.iota(jnp.int32, experts)
    member = (routes[:, None] == labels[None, :]).astype(jnp.int32)
    layout = placement(member, capacity).reshape(experts, capacity, tok_dev)
    cotangent_wide = cotangent.astype(jnp.float32)
    out_grad = (combine[:, None] * cotangent_wide).astype(jnp.bfloat16)
    layouts = [
        layout[:, c * chunk_slots : (c + 1) * chunk_slots].reshape(-1, tok_dev)
        for c in range(chunks)
    ]
    tok_in = [group_rows(exchange(spread(lay, tokens), experts, model_width)) for lay in layouts]
    cot_in = [group_rows(exchange(spread(lay, out_grad), experts, model_width)) for lay in layouts]
    expert_out = None
    input_grad = None
    for c in range(chunks):
        gate_act, up_act, part = forward_rows(tok_in[c], weights)
        out_back = exchange(group_sum(part), experts, model_width)
        piece = collect(layouts[c], out_back)
        expert_out = piece if expert_out is None else expert_out + piece
        grad_part = backward_rows(cot_in[c], gate_act, up_act, weights)
        grad_back = exchange(group_sum(grad_part), experts, model_width)
        piece = collect(layouts[c], grad_back)
        input_grad = piece if input_grad is None else input_grad + piece
    combined = (combine[:, None] * expert_out).astype(jnp.bfloat16)
    combine_grad = jnp.sum(expert_out * cotangent_wide, 1)
    token_grad = input_grad.astype(jnp.bfloat16)
    return (combined, token_grad, combine_grad)


def solution(mesh):
    return jax.shard_map(
        shards,
        mesh=mesh,
        in_specs=(
            P(("dp", "expert"), None),
            P(("dp", "expert"), None),
            P(("dp", "expert")),
            P(("dp", "expert")),
            P("expert", None, "dp", None),
        ),
        out_specs=(P(("dp", "expert"), None), P(("dp", "expert"), None), P(("dp", "expert"))),
        check_vma=False,
    )
```

profile of v0, /device:TPU:1, one launch (start us, length us, event | category | flops | bytes accessed | tf_op | source)
XLA Modules:
  0.0 472.8 jit_solution(6738018536119864457)
XLA Ops:
  12.2 26.4 %all_to_all.40 = bf16[32,4,4096]{2,1,0:T(4,128)(2,1)} all-to-all(bf16[32,4,4096]{2,1,0:T(4,128)(2,1)S(1)} %reshape.93), channel_id=1, replica_groups=mesh['dp'=4,'expert'=32] {'expert'}, dimensions={0} | all-to-all | bytes 2097152 | tf_op jit(solution)/shard_map/all_to_all | solution.py:35
  38.7 2.1 reshape.94
  42.6 20.9 %all_to_all.41 = bf16[32,4,4096]{2,1,0:T(4,128)(2,1)S(1)} all-to-all(bf16[32,4,4096]{2,1,0:T(4,128)(2,1)} %reshape.99), channel_id=1, replica_groups=mesh['dp'=4,'expert'=32] {'expert'}, dimensions={0} | all-to-all | bytes 2097152 | tf_op jit(solution)/shard_map/all_to_all | solution.py:35
  65.6 20.7 %all_to_all.42 = bf16[32,4,4096]{2,1,0:T(4,128)(2,1)S(1)} all-to-all(bf16[32,4,4096]{2,1,0:T(4,128)(2,1)S(1)} %reshape.89), channel_id=1, replica_groups=mesh['dp'=4,'expert'=32] {'expert'}, dimensions={0} | all-to-all | bytes 2097152 | tf_op jit(solution)/shard_map/all_to_all | solution.py:35
  88.3 20.7 %all_to_all.43 = bf16[32,4,4096]{2,1,0:T(4,128)(2,1)S(1)} all-to-all(bf16[32,4,4096]{2,1,0:T(4,128)(2,1)S(1)} %reshape.96), channel_id=1, replica_groups=mesh['dp'=4,'expert'=32] {'expert'}, dimensions={0} | all-to-all | bytes 2097152 | tf_op jit(solution)/shard_map/all_to_all | solution.py:35
  110.2 8.8 %fusion.32 = f32[2,512,384]{2,1,0:T(8,128)} fusion(bf16[1,3,384,4096]{3,2,1,0:T(8,128)(2,1)} %param.9, bf16[512,4096]{1,0:T(8,128)(2,1)} %all-gather.7.cloned.1.call-done), kind=kOutput, calls=%fused_computation.43 | convolution fusion | flops 3221225472 | bytes 12058624 | tf_op jit(solution)/shard_map/rd,kfd->krf/dot_general | solution.py:41
  119.0 18.0 %all-gather.11.cloned.1.call-done = bf16[512,4096]{1,0:T(8,128)(2,1)} async-done(((bf16[128,4096]{1,0:T(8,128)(2,1)}), bf16[512,4096]{1,0:T(8,128)(2,1)}) %all-gather.11.cloned.1.call-update) | async-done | bytes 4194320 | tf_op jit(solution)/shard_map/all_gather | solution.py:27
  137.0 6.0 %fusion.72 = (bf16[1,512,384]{2,1,0:T(8,128)(2,1)S(1)}, bf16[1,512,384]{2,1,0:T(8,128)(2,1)S(1)}) fusion(f32[2,512,384]{2,1,0:T(8,128)} %fusion.32, bf16[512,4096]{1,0:T(8,128)(2,1)} %all-gather.11.cloned.1.call-done, bf16[1,3,384,4096]{3,2,1,0:T(8,128)(2,1)} %param.9), kind=kOutput, calls=%fused_computation.87 | convolution fusion | flops 1613168640 | bytes 9699328 | tf_op jit(solution)/shard_map/dot_general | solution.py:50
  143.0 7.7 %bitcast_convert_fusion = bf16[512,4096]{1,0:T(8,128)(2,1)} fusion(bf16[1,3,384,4096]{3,2,1,0:T(8,128)(2,1)} %param.9, bf16[1,512,384]{2,1,0:T(8,128)(2,1)S(1)} %get-tuple-element.9, bf16[1,512,384]{2,1,0:T(8,128)(2,1)S(1)} %get-tuple-element.8), kind=kOutput, calls=%fused_computation | convolution fusion | flops 3223715840 | bytes 11272192 | tf_op jit(solution)/shard_map/krf,kfd->rd/dot_general | solution.py:59
  151.0 36.9 %all-gather.5.cloned.1.call-done = bf16[512,4096]{1,0:T(8,128)(2,1)} async-done(((bf16[128,4096]{1,0:T(8,128)(2,1)}), bf16[512,4096]{1,0:T(8,128)(2,1)}) %all-gather.5.cloned.1.call-update) | async-done | bytes 4194320 | tf_op jit(solution)/shard_map/all_gather | solution.py:27
  187.9 8.7 %fusion.27 = f32[2,512,384]{2,1,0:T(8,128)} fusion(bf16[1,3,384,4096]{3,2,1,0:T(8,128)(2,1)} %param.9, bf16[512,4096]{1,0:T(8,128)(2,1)} %all-gather.5.cloned.1.call-done), kind=kOutput, calls=%fused_computation.42 | convolution fusion | flops 3221225472 | bytes 12058624 | tf_op jit(solution)/shard_map/rd,kfd->krf/dot_general | solution.py:41
  196.6 41.5 %all-gather.9.cloned.1.call-done = bf16[512,4096]{1,0:T(8,128)(2,1)} async-done(((bf16[128,4096]{1,0:T(8,128)(2,1)}), bf16[512,4096]{1,0:T(8,128)(2,1)}) %all-gather.9.cloned.1.call-update) | async-done | bytes 4194320 | tf_op jit(solution)/shard_map/all_gather | solution.py:27
  238.0 6.0 %fusion.71 = (bf16[1,512,384]{2,1,0:T(8,128)(2,1)S(1)}, bf16[1,512,384]{2,1,0:T(8,128)(2,1)S(1)}) fusion(f32[2,512,384]{2,1,0:T(8,128)} %fusion.27, bf16[512,4096]{1,0:T(8,128)(2,1)} %all-gather.9.cloned.1.call-done, bf16[1,3,384,4096]{3,2,1,0:T(8,128)(2,1)} %param.9), kind=kOutput, calls=%fused_computation.86 | convolution fusion | flops 1613168640 | bytes 9699328 | tf_op jit(solution)/shard_map/dot_general | solution.py:50
  244.0 7.7 %bitcast_convert_fusion.1 = bf16[512,4096]{1,0:T(8,128)(2,1)} fusion(bf16[1,3,384,4096]{3,2,1,0:T(8,128)(2,1)} %param.9, bf16[1,512,384]{2,1,0:T(8,128)(2,1)S(1)} %get-tuple-element.7, bf16[1,512,384]{2,1,0:T(8,128)(2,1)S(1)} %get-tuple-element.6), kind=kOutput, calls=%fused_computation.1 | convolution fusion | flops 3223715840 | bytes 11272192 | tf_op jit(solution)/shard_map/krf,kfd->rd/dot_general | solution.py:59
  251.8 6.7 %convolution_convert_fusion = bf16[512,4096]{1,0:T(8,128)(2,1)} fusion(bf16[1,3,384,4096]{3,2,1,0:T(8,128)(2,1)} %param.9, f32[2,512,384]{2,1,0:T(8,128)} %fusion.32), kind=kOutput, calls=%fused_computation.8 | convolution fusion | flops 1613889536 | bytes 8912896 | tf_op jit(solution)/shard_map/dot_general | solution.py:45
  258.6 6.8 %convolution_convert_fusion.1 = bf16[512,4096]{1,0:T(8,128)(2,1)} fusion(bf16[1,3,384,4096]{3,2,1,0:T(8,128)(2,1)} %param.9, f32[2,512,384]{2,1,0:T(8,128)} %fusion.27), kind=kOutput, calls=%fused_computation.9 | convolution fusion | flops 1613889536 | bytes 8912896 | tf_op jit(solution)/shard_map/dot_general | solution.py:45
  265.5 22.0 %reduce-scatter.11.cloned.1.call-done = bf16[128,4096]{1,0:T(8,128)(2,1)} async-done(((bf16[512,4096]{1,0:T(8,128)(2,1)}), bf16[128,4096]{1,0:T(8,128)(2,1)}) %reduce-scatter.11.cloned.1.call-update) | async-done | bytes 1048592 | tf_op jit(solution)/shard_map/reduce_scatter | solution.py:31
  287.5 2.2 reshape.101
  289.7 7.6 %all-to-all-start.7 = ((bf16[32,4,4096]{2,1,0:T(4,128)(2,1)}), bf16[32,4,4096]{2,1,0:T(4,128)(2,1)S(1)}, u32[]{:S(2)}, u32[]{:S(2)}) async-start(bf16[32,4,4096]{2,1,0:T(4,128)(2,1)} %reshape.101), calls=%async_computation.11 | async-start | bytes 2097152 | tf_op jit(solution)/shard_map/all_to_all | solution.py:35
  297.4 39.1 %reduce-scatter.9.cloned.1.call-done = bf16[128,4096]{1,0:T(8,128)(2,1)} async-done(((bf16[512,4096]{1,0:T(8,128)(2,1)}), bf16[128,4096]{1,0:T(8,128)(2,1)}) %reduce-scatter.9.cloned.1.call-update) | async-done | bytes 1048592 | tf_op jit(solution)/shard_map/reduce_scatter | solution.py:31
  336.5 2.2 reshape.98
  338.7 7.7 %all-to-all-start.5 = ((bf16[32,4,4096]{2,1,0:T(4,128)(2,1)}), bf16[32,4,4096]{2,1,0:T(4,128)(2,1)S(1)}, u32[]{:S(2)}, u32[]{:S(2)}) async-start(bf16[32,4,4096]{2,1,0:T(4,128)(2,1)} %reshape.98), calls=%async_computation.8 | async-start | bytes 2097152 | tf_op jit(solution)/shard_map/all_to_all | solution.py:35
  346.4 39.0 %reduce-scatter.7.cloned.1.call-done = bf16[128,4096]{1,0:T(8,128)(2,1)} async-done(((bf16[512,4096]{1,0:T(8,128)(2,1)}), bf16[128,4096]{1,0:T(8,128)(2,1)}) %reduce-scatter.7.cloned.1.call-update) | async-done | bytes 1048592 | tf_op jit(solution)/shard_map/reduce_scatter | solution.py:31
  385.4 2.2 reshape.95
  388.7 7.7 %all-to-all-start.3 = ((bf16[32,4,4096]{2,1,0:T(4,128)(2,1)}), bf16[32,4,4096]{2,1,0:T(4,128)(2,1)S(1)}, u32[]{:S(2)}, u32[]{:S(2)}) async-start(bf16[32,4,4096]{2,1,0:T(4,128)(2,1)} %reshape.95), calls=%async_computation.5 | async-start | bytes 2097152 | tf_op jit(solution)/shard_map/all_to_all | solution.py:35
  396.3 38.2 %reduce-scatter.5.cloned.1.call-done = bf16[128,4096]{1,0:T(8,128)(2,1)} async-done(((bf16[512,4096]{1,0:T(8,128)(2,1)}), bf16[128,4096]{1,0:T(8,128)(2,1)}) %reduce-scatter.5.cloned.1.call-update) | async-done | bytes 1048592 | tf_op jit(solution)/shard_map/reduce_scatter | solution.py:31
  434.5 2.2 reshape.91
  436.8 7.7 %all-to-all-start.1 = ((bf16[32,4,4096]{2,1,0:T(4,128)(2,1)}), bf16[32,4,4096]{2,1,0:T(4,128)(2,1)}, u32[]{:S(2)}, u32[]{:S(2)}) async-start(bf16[32,4,4096]{2,1,0:T(4,128)(2,1)} %reshape.91), calls=%async_computation.2 | async-start | bytes 2097152 | tf_op jit(solution)/shard_map/all_to_all | solution.py:35
  445.4 2.2 convolution_bitcast_fusion.2
  447.6 1.9 fusion.8
  449.5 11.9 %all-to-all-done.1 = bf16[32,4,4096]{2,1,0:T(4,128)(2,1)} async-done(((bf16[32,4,4096]{2,1,0:T(4,128)(2,1)}), bf16[32,4,4096]{2,1,0:T(4,128)(2,1)}, u32[]{:S(2)}, u32[]{:S(2)}) %all-to-all-start.1) | async-done | bytes 1048608 | tf_op jit(solution)/shard_map/all_to_all | solution.py:35
  461.4 4.6 fusion.22
  (54 shorter events, 14.4 us)
Async XLA Ops:
  7.2 2.1 copy-start
  7.2 103.0 %all-gather.7.cloned.1.call-start = ((), (), s32[]{:S(2)}) async-start(), calls=%async_computation.14 | async-start | bytes 5242880 | tf_op jit(solution)/shard_map/all_gather | solution.py:27
  10.7 30.2 %copy-start.2 = (bf16[128,4096]{1,0:T(8,128)(2,1)S(1)}, bf16[128,4096]{1,0:T(8,128)(2,1)}, u32[]{:S(2)}) copy-start(bf16[128,4096]{1,0:T(8,128)(2,1)} %param.6) | copy-start | bytes 3145732
  10.7 30.2 %copy-start.5 = (f32[128]{0:T(128)S(1)}, f32[128]{0:T(128)}, u32[]{:S(2)}) copy-start(f32[128]{0:T(128)} %param.8) | copy-start | bytes 1540
  40.8 96.2 %all-gather.11.cloned.1.call-start = ((), (), s32[]{:S(2)}) async-start(), calls=%async_computation.18 | async-start | bytes 5242880 | tf_op jit(solution)/shard_map/all_gather | solution.py:27
  64.6 123.3 %all-gather.5.cloned.1.call-start = ((), (), s32[]{:S(2)}) async-start(), calls=%async_computation.12 | async-start | bytes 5242880 | tf_op jit(solution)/shard_map/all_gather | solution.py:27
  87.3 150.7 %all-gather.9.cloned.1.call-start = ((), (), s32[]{:S(2)}) async-start(), calls=%async_computation.16 | async-start | bytes 5242880 | tf_op jit(solution)/shard_map/all_gather | solution.py:27
  110.1 177.4 %reduce-scatter.11.cloned.1.call-start = ((), (), s32[]{:S(2)}) async-start(), calls=%async_computation.19 | async-start | bytes 5242880 | tf_op jit(solution)/shard_map/reduce_scatter | solution.py:31
  150.8 185.7 %reduce-scatter.9.cloned.1.call-start = ((), (), s32[]{:S(2)}) async-start(), calls=%async_computation.17 | async-start | bytes 5242880 | tf_op jit(solution)/shard_map/reduce_scatter | solution.py:31
  251.8 133.6 %reduce-scatter.7.cloned.1.call-start = ((), (), s32[]{:S(2)}) async-start(), calls=%async_computation.15 | async-start | bytes 5242880 | tf_op jit(solution)/shard_map/reduce_scatter | solution.py:31
  258.6 175.9 %reduce-scatter.5.cloned.1.call-start = ((), (), s32[]{:S(2)}) async-start(), calls=%async_computation.13 | async-start | bytes 5242880 | tf_op jit(solution)/shard_map/reduce_scatter | solution.py:31
  289.7 49.0 %all-to-all-start.7 = ((bf16[32,4,4096]{2,1,0:T(4,128)(2,1)}), bf16[32,4,4096]{2,1,0:T(4,128)(2,1)S(1)}, u32[]{:S(2)}, u32[]{:S(2)}) async-start(bf16[32,4,4096]{2,1,0:T(4,128)(2,1)} %reshape.101), calls=%async_computation.11 | async-start | bytes 2097152 | tf_op jit(solution)/shard_map/all_to_all | solution.py:35
  338.7 48.9 %all-to-all-start.5 = ((bf16[32,4,4096]{2,1,0:T(4,128)(2,1)}), bf16[32,4,4096]{2,1,0:T(4,128)(2,1)S(1)}, u32[]{:S(2)}, u32[]{:S(2)}) async-start(bf16[32,4,4096]{2,1,0:T(4,128)(2,1)} %reshape.98), calls=%async_computation.8 | async-start | bytes 2097152 | tf_op jit(solution)/shard_map/all_to_all | solution.py:35
  387.6 1.0 copy-start.3
  388.7 48.1 %all-to-all-start.3 = ((bf16[32,4,4096]{2,1,0:T(4,128)(2,1)}), bf16[32,4,4096]{2,1,0:T(4,128)(2,1)S(1)}, u32[]{:S(2)}, u32[]{:S(2)}) async-start(bf16[32,4,4096]{2,1,0:T(4,128)(2,1)} %reshape.95), calls=%async_computation.5 | async-start | bytes 2097152 | tf_op jit(solution)/shard_map/all_to_all | solution.py:35
  436.8 24.7 %all-to-all-start.1 = ((bf16[32,4,4096]{2,1,0:T(4,128)(2,1)}), bf16[32,4,4096]{2,1,0:T(4,128)(2,1)}, u32[]{:S(2)}, u32[]{:S(2)}) async-start(bf16[32,4,4096]{2,1,0:T(4,128)(2,1)} %reshape.91), calls=%async_computation.2 | async-start | bytes 2097152 | tf_op jit(solution)/shard_map/all_to_all | solution.py:35
  444.5 3.2 copy-start.4
  445.4 20.6 %copy-start.1 = (bf16[128,4096]{1,0:T(8,128)(2,1)S(1)}, bf16[128,4096]{1,0:T(8,128)(2,1)}, u32[]{:S(2)}) copy-start(bf16[128,4096]{1,0:T(8,128)(2,1)} %param.5) | copy-start | bytes 3145732
Sparse Core Ops, SparseCore 0:
  40.9 45.7 all-gather.6
  88.4 48.5 all-gather.10
  139.3 48.5 all-gather.4
  189.4 48.5 all-gather.8
  240.3 47.1 reduce-scatter.10
  289.9 46.5 reduce-scatter.8
  338.9 46.4 reduce-scatter.6
  387.9 46.5 reduce-scatter.4
where the time goes:
time: 474 us; the launch traced here: 473 us
  waiting for transfers between devices  247 us (52%)
  blocking collectives  88.6 us (19%)
  matrix products  70.8 us (15%)
  starting transfers between devices  31.2 us (7%)
  local copies, waits for them, and re-layouts  19.1 us (4%)
  between operations  14.4 us (3%)
    reduce_scatter x4, waiting for transfers between devices, group_sum(): lax.psum_scatter(values.astype(jnp.bfloat16), 'dp', scatter_dimension=0,...  138 us
    all_gather x4, waiting for transfers between devices, group_rows(): return lax.all_gather(values, 'dp', axis=0, tiled=True)  96.4 us
    all_to_all x4, blocking collectives, exchange(): lax.all_to_all(rows.reshape(experts, -1, model_width), 'expert', split_ax...  88.6 us
    all_to_all x4, starting transfers between devices, exchange(): lax.all_to_all(rows.reshape(experts, -1, model_width), 'expert', split_ax...  30.7 us
    dot_general x2, matrix products, forward_rows(): jnp.einsum('rd,kfd->krf', row_block, matrices[:2], preferred_element_type...  17.4 us
    dot_general x2, matrix products, backward_rows(): jnp.einsum('krf,kfd->rd', both_grads, matrices[:2], preferred_element_typ...  15.5 us
    dot_general x2, matrix products, forward_rows(): jnp.dot(hidden, matrices[2], preferred_element_type=jnp.float32)  13.5 us
    reshape x8, local copies, waits for them, and re-layouts, exchange(): rows.reshape(experts, -1, model_width)  12.6 us
  transfers between devices with their start and end apart: 12, of which 8 were waited for; matrix products, arithmetic and copies ran while one was open for 17% of the time, Pallas kernels for 0%

commit v1 on v0

--- a/solution.py
+++ b/solution.py
@@ -1,7 +1,34 @@
+import functools
 import jax
 import jax.numpy as jnp
 from jax import lax
 from jax.sharding import PartitionSpec as P
+
+
+def _view_pages(base_x, mesh_ax):
+    state_next = lax.axis_index(mesh_ax)
+    work_now = lax.axis_size(mesh_ax)
+    x_new, y1, current_value = (work_now, state_next, base_x.shape[0])
+    windows = tuple(((k, (k + 1) % x_new) for k in range(x_new)))
+    e_next = jnp.zeros((*base_x.shape[:0], x_new * current_value, *base_x.shape[1:]), base_x.dtype)
+    e_next = lax.dynamic_update_slice_in_dim(e_next, base_x, y1 * current_value, axis=0)
+    far_arr = y = base_x
+    tray = tuple(((k, (k - 1) % x_new) for k in range(x_new)))
+    y_new = x_new // 2
+    for idx in range(1, y_new + 1):
+        far_arr = lax.ppermute(far_arr, mesh_ax, windows)
+        e_next = lax.dynamic_update_slice_in_dim(
+            e_next, far_arr, (y1 - idx) % x_new * current_value, axis=0
+        )
+        if idx < x_new - y_new:
+            y = lax.ppermute(y, mesh_ax, tray)
+            e_next = lax.dynamic_update_slice_in_dim(
+                e_next, y, (y1 + idx) % x_new * current_value, axis=0
+            )
+    return e_next
+
+
+expand_strings = functools.partial(_view_pages, mesh_ax="dp")
 
 
 def placement(member, slot_count):
@@ -24,7 +51,7 @@
 
 
 def group_rows(values):
-    return lax.all_gather(values, "dp", axis=0, tiled=True)
+    return expand_strings(values)
 
 
 def group_sum(values):

time: 474 us -> 510 us (1.076)
  waiting for transfers between devices: 247 us -> 287 us
  matrix products: 70.8 us -> 51.4 us
  blocking collectives: 88.6 us -> 98.9 us
    ppermute x0 -> x12, waiting for transfers between devices: none -> 231 us  [the longest x8 231 us: _view_pages(): far_arr = lax.ppermute(far_arr, mesh_ax, windows)]
    reduce_scatter x4, waiting for transfers between devices: 138 us -> 0.08 us  [group_sum(): lax.psum_scatter(values.astype(jnp.bfloat16), 'dp', scatter_dimension=0,...]
    all_gather x4 -> x0, waiting for transfers between devices: 96.4 us -> none  [group_rows(): return lax.all_gather(values, 'dp', axis=0, tiled=True)]
    all_to_all x4, waiting for transfers between devices: 11.9 us -> 55 us  [exchange(): lax.all_to_all(rows.reshape(experts, -1, model_width), 'expert', split_ax...]
    ppermute x0 -> x12, starting transfers between devices: none -> 11.1 us  [the longest x4 9.47 us: _view_pages(): y = lax.ppermute(y, mesh_ax, tray)]
    all_to_all x4, blocking collectives: 88.6 us -> 98.9 us  [exchange(): lax.all_to_all(rows.reshape(experts, -1, model_width), 'expert', split_ax...]
    all_to_all x4, starting transfers between devices: 30.7 us -> 20.7 us  [exchange(): lax.all_to_all(rows.reshape(experts, -1, model_width), 'expert', split_ax...]
    dot_general x2, matrix products: 17.4 us -> 10.2 us  [forward_rows(): jnp.einsum('rd,kfd->krf', row_block, matrices[:2], preferred_element_type...]
  transfers between devices with their start and end apart: 12 -> 20, of which waited for: 8 -> 12; matrix products, arithmetic and copies ran while one was open for 17% -> 11% of each run, Pallas kernels for 0% -> 0%
where the time goes in v1:
time: 510 us; the launch traced here: 509 us
  waiting for transfers between devices  287 us (56%)
  blocking collectives  98.9 us (19%)
  matrix products  51.4 us (10%)
  starting transfers between devices  32 us (6%)
  local copies, waits for them, and re-layouts  23.8 us (5%)
  between operations  14.4 us (3%)
    ppermute x8, waiting for transfers between devices, _view_pages(): far_arr = lax.ppermute(far_arr, mesh_ax, windows)  231 us
    all_to_all x4, blocking collectives, exchange(): lax.all_to_all(rows.reshape(experts, -1, model_width), 'expert', split_ax...  98.9 us
    all_to_all x4, waiting for transfers between devices, exchange(): lax.all_to_all(rows.reshape(experts, -1, model_width), 'expert', split_ax...  55 us
    all_to_all x4, starting transfers between devices, exchange(): lax.all_to_all(rows.reshape(experts, -1, model_width), 'expert', split_ax...  20.7 us
    reshape x8, local copies, waits for them, and re-layouts, exchange(): rows.reshape(experts, -1, model_width)  10.7 us
    dot_general x2, matrix products, forward_rows(): jnp.dot(hidden, matrices[2], preferred_element_type=jnp.float32)  10.6 us
    dot_general x2, matrix products, forward_rows(): jnp.einsum('rd,kfd->krf', row_block, matrices[:2], preferred_element_type...  10.2 us
  transfers between devices with their start and end apart: 20, of which 12 were waited for; matrix products, arithmetic and copies ran while one was open for 11% of the time, Pallas kernels for 0%

profile of v1, /device:TPU:1, one launch (start us, length us, event | category | flops | bytes accessed | tf_op | source)
XLA Modules:
  0.0 509.0 jit_solution(14484432593515155934)
XLA Ops:
  10.2 26.3 %all_to_all.40 = bf16[32,4,4096]{2,1,0:T(4,128)(2,1)S(1)} all-to-all(bf16[32,4,4096]{2,1,0:T(4,128)(2,1)S(1)} %reshape.93), channel_id=1, replica_groups=mesh['dp'=4,'expert'=32] {'expert'}, dimensions={0} | all-to-all | bytes 2097152 | tf_op jit(solution)/shard_map/all_to_all | solution.py:62
  39.5 23.2 %collective-permute-done.3 = bf16[128,4096]{1,0:T(8,128)(2,1)S(1)} collective-permute-done((bf16[128,4096]{1,0:T(8,128)(2,1)S(1)}, bf16[128,4096]{1,0:T(8,128)(2,1)S(1)}, u32[]{:S(2)}, u32[]{:S(2)}) %collective-permute-start.3) | collective-permute-done | bytes 1048608 | tf_op jit(solution)/shard_map/ppermute | solution.py:19
  65.2 22.4 %collective-permute-done.5 = bf16[128,4096]{1,0:T(8,128)(2,1)S(1)} collective-permute-done((bf16[128,4096]{1,0:T(8,128)(2,1)S(1)}, bf16[128,4096]{1,0:T(8,128)(2,1)S(1)}, u32[]{:S(2)}, u32[]{:S(2)}) %collective-permute-start.5) | collective-permute-done | bytes 1048608 | tf_op jit(solution)/shard_map/ppermute | solution.py:19
  87.7 3.5 fusion.32
  92.3 4.3 convolution_convert_fusion
  97.6 22.1 %all_to_all.41 = bf16[32,4,4096]{2,1,0:T(4,128)(2,1)S(1)} all-to-all(bf16[32,4,4096]{2,1,0:T(4,128)(2,1)S(1)} %reshape.89), channel_id=1, replica_groups=mesh['dp'=4,'expert'=32] {'expert'}, dimensions={0} | all-to-all | bytes 2097152 | tf_op jit(solution)/shard_map/all_to_all | solution.py:62
  120.1 2.7 collective-permute-start.1
  122.8 38.8 %collective-permute-done = bf16[128,4096]{1,0:T(8,128)(2,1)S(1)} collective-permute-done((bf16[128,4096]{1,0:T(8,128)(2,1)S(1)}, bf16[128,4096]{1,0:T(8,128)(2,1)S(1)}, u32[]{:S(2)}, u32[]{:S(2)}) %collective-permute-start) | collective-permute-done | bytes 1048608 | tf_op jit(solution)/shard_map/ppermute | solution.py:19
  162.4 24.5 %collective-permute-done.2 = bf16[128,4096]{1,0:T(8,128)(2,1)S(1)} collective-permute-done((bf16[128,4096]{1,0:T(8,128)(2,1)S(1)}, bf16[128,4096]{1,0:T(8,128)(2,1)S(1)}, u32[]{:S(2)}, u32[]{:S(2)}) %collective-permute-start.2) | collective-permute-done | bytes 1048608 | tf_op jit(solution)/shard_map/ppermute | solution.py:19
  187.0 6.7 %fusion.27 = f32[2,512,384]{2,1,0:T(8,128)S(1)} fusion(bf16[1,3,384,4096]{3,2,1,0:T(8,128)(2,1)} %param.9, bf16[512,4096]{1,0:T(8,128)(2,1)S(1)} %constant_dynamic-update-slice_fusion.11), kind=kOutput, calls=%fused_computation.42 | convolution fusion | flops 3221225472 | bytes 12058624 | tf_op jit(solution)/shard_map/rd,kfd->krf/dot_general | solution.py:68
  194.9 6.3 %convolution_convert_fusion.1 = bf16[512,4096]{1,0:T(8,128)(2,1)} fusion(bf16[1,3,384,4096]{3,2,1,0:T(8,128)(2,1)} %param.9, f32[2,512,384]{2,1,0:T(8,128)S(1)} %fusion.27), kind=kOutput, calls=%fused_computation.9 | convolution fusion | flops 1613889536 | bytes 8912896 | tf_op jit(solution)/shard_map/dot_general | solution.py:72
  203.4 25.2 %all_to_all.42 = bf16[32,4,4096]{2,1,0:T(4,128)(2,1)} all-to-all(bf16[32,4,4096]{2,1,0:T(4,128)(2,1)S(1)} %reshape.99), channel_id=1, replica_groups=mesh['dp'=4,'expert'=32] {'expert'}, dimensions={0} | all-to-all | bytes 2097152 | tf_op jit(solution)/shard_map/all_to_all | solution.py:62
  232.7 36.2 %collective-permute-done.9 = bf16[128,4096]{1,0:T(8,128)(2,1)S(1)} collective-permute-done((bf16[128,4096]{1,0:T(8,128)(2,1)S(1)}, bf16[128,4096]{1,0:T(8,128)(2,1)S(1)}, u32[]{:S(2)}, u32[]{:S(2)}) %collective-permute-start.9) | collective-permute-done | bytes 1048608 | tf_op jit(solution)/shard_map/ppermute | solution.py:19
  269.9 24.5 %collective-permute-done.11 = bf16[128,4096]{1,0:T(8,128)(2,1)S(1)} collective-permute-done((bf16[128,4096]{1,0:T(8,128)(2,1)S(1)}, bf16[128,4096]{1,0:T(8,128)(2,1)S(1)}, u32[]{:S(2)}, u32[]{:S(2)}) %collective-permute-start.11) | collective-permute-done | bytes 1048608 | tf_op jit(solution)/shard_map/ppermute | solution.py:19
  294.5 4.5 fusion.72
  299.1 5.0 bitcast_convert_fusion
  305.1 25.2 %all_to_all.43 = bf16[32,4,4096]{2,1,0:T(4,128)(2,1)} all-to-all(bf16[32,4,4096]{2,1,0:T(4,128)(2,1)S(1)} %reshape.96), channel_id=1, replica_groups=mesh['dp'=4,'expert'=32] {'expert'}, dimensions={0} | all-to-all | bytes 2097152 | tf_op jit(solution)/shard_map/all_to_all | solution.py:62
  331.8 2.7 collective-permute-start.7
  334.5 37.4 %collective-permute-done.6 = bf16[128,4096]{1,0:T(8,128)(2,1)S(1)} collective-permute-done((bf16[128,4096]{1,0:T(8,128)(2,1)S(1)}, bf16[128,4096]{1,0:T(8,128)(2,1)S(1)}, u32[]{:S(2)}, u32[]{:S(2)}) %collective-permute-start.6) | collective-permute-done | bytes 1048608 | tf_op jit(solution)/shard_map/ppermute | solution.py:19
  372.7 24.5 %collective-permute-done.8 = bf16[128,4096]{1,0:T(8,128)(2,1)S(1)} collective-permute-done((bf16[128,4096]{1,0:T(8,128)(2,1)S(1)}, bf16[128,4096]{1,0:T(8,128)(2,1)S(1)}, u32[]{:S(2)}, u32[]{:S(2)}) %collective-permute-start.8) | collective-permute-done | bytes 1048608 | tf_op jit(solution)/shard_map/ppermute | solution.py:19
  397.4 4.5 fusion.71
  402.0 5.0 bitcast_convert_fusion.1
  409.2 8.3 %all-to-all-start.3 = ((bf16[32,4,4096]{2,1,0:T(4,128)(2,1)}), bf16[32,4,4096]{2,1,0:T(4,128)(2,1)S(1)}, u32[]{:S(2)}, u32[]{:S(2)}) async-start(bf16[32,4,4096]{2,1,0:T(4,128)(2,1)} %reshape.95), calls=%async_computation.5 | async-start | bytes 2097152 | tf_op jit(solution)/shard_map/all_to_all | solution.py:62
  419.9 14.6 %all-to-all-done.3 = bf16[32,4,4096]{2,1,0:T(4,128)(2,1)S(1)} async-done(((bf16[32,4,4096]{2,1,0:T(4,128)(2,1)}), bf16[32,4,4096]{2,1,0:T(4,128)(2,1)S(1)}, u32[]{:S(2)}, u32[]{:S(2)}) %all-to-all-start.3) | async-done | bytes 1048608 | tf_op jit(solution)/shard_map/all_to_all | solution.py:62
  434.5 4.0 all-to-all-start.1
  440.8 14.6 %all-to-all-done.1 = bf16[32,4,4096]{2,1,0:T(4,128)(2,1)S(1)} async-done(((bf16[32,4,4096]{2,1,0:T(4,128)(2,1)}), bf16[32,4,4096]{2,1,0:T(4,128)(2,1)S(1)}, u32[]{:S(2)}, u32[]{:S(2)}) %all-to-all-start.1) | async-done | bytes 1048608 | tf_op jit(solution)/shard_map/all_to_all | solution.py:62
  456.4 4.0 all-to-all-start.7
  462.6 14.6 %all-to-all-done.7 = bf16[32,4,4096]{2,1,0:T(4,128)(2,1)S(1)} async-done(((bf16[32,4,4096]{2,1,0:T(4,128)(2,1)}), bf16[32,4,4096]{2,1,0:T(4,128)(2,1)S(1)}, u32[]{:S(2)}, u32[]{:S(2)}) %all-to-all-start.7) | async-done | bytes 1048608 | tf_op jit(solution)/shard_map/all_to_all | solution.py:62
  477.2 4.4 all-to-all-start.5
  484.9 2.7 fusion.22
  487.6 11.1 %all-to-all-done.5 = bf16[32,4,4096]{2,1,0:T(4,128)(2,1)} async-done(((bf16[32,4,4096]{2,1,0:T(4,128)(2,1)}), bf16[32,4,4096]{2,1,0:T(4,128)(2,1)}, u32[]{:S(2)}, u32[]{:S(2)}) %all-to-all-start.5) | async-done | bytes 1048608 | tf_op jit(solution)/shard_map/all_to_all | solution.py:62
  498.7 3.8 fusion.8
  (110 shorter events, 36.8 us)
Async XLA Ops:
  7.2 2.1 copy-start
  7.2 399.8 %reduce-scatter.7.cloned.1.call-start = ((), (), s32[]{:S(2)}) async-start(), calls=%async_computation.13 | async-start | bytes 5242880 | tf_op jit(solution)/shard_map/reduce_scatter | solution.py:58
  36.7 25.9 %collective-permute-start.3 = (bf16[128,4096]{1,0:T(8,128)(2,1)S(1)}, bf16[128,4096]{1,0:T(8,128)(2,1)S(1)}, u32[]{:S(2)}, u32[]{:S(2)}) collective-permute-start(bf16[128,4096]{1,0:T(8,128)(2,1)S(1)} %reshape.94), channel_id=1, source_target_pairs={{0,32},{32,64},{64,96},{96,0},{1,33},{33,65},{65,97},{97,1},{2,34}... | collective-permute-start | bytes 3145736 | tf_op jit(solution)/shard_map/ppermute | solution.py:19
  38.0 25.5 %collective-permute-start.4 = (bf16[128,4096]{1,0:T(8,128)(2,1)S(1)}, bf16[128,4096]{1,0:T(8,128)(2,1)}, u32[]{:S(2)}, u32[]{:S(2)}) collective-permute-start(bf16[128,4096]{1,0:T(8,128)(2,1)S(1)} %reshape.94), channel_id=1, source_target_pairs={{0,96},{32,0},{64,32},{96,64},{1,97},{33,1},{65,33},{97,65},{2,98}... | collective-permute-start | bytes 3145736 | tf_op jit(solution)/shard_map/ppermute | solution.py:24
  62.6 24.9 %collective-permute-start.5 = (bf16[128,4096]{1,0:T(8,128)(2,1)S(1)}, bf16[128,4096]{1,0:T(8,128)(2,1)S(1)}, u32[]{:S(2)}, u32[]{:S(2)}) collective-permute-start(bf16[128,4096]{1,0:T(8,128)(2,1)S(1)} %collective-permute-done.3), channel_id=1, source_target_pairs={{0,32},{32,64},{64,96},{96,0},{1,33},{33,65},{65,97},{97,1},{2,34}... | collective-permute-start | bytes 3145736 | tf_op jit(solution)/shard_map/ppermute | solution.py:19
  62.7 24.9 %copy-start.6 = (bf16[1,3,384,4096]{3,2,1,0:T(8,128)(2,1)S(1)}, bf16[1,3,384,4096]{3,2,1,0:T(8,128)(2,1)}, u32[]{:S(2)}) copy-start(bf16[1,3,384,4096]{3,2,1,0:T(8,128)(2,1)} %param.9) | copy-start | bytes 28311556
  96.7 320.9 %reduce-scatter.5.cloned.1.call-start = ((), (), s32[]{:S(2)}) async-start(), calls=%async_computation.12 | async-start | bytes 5242880 | tf_op jit(solution)/shard_map/reduce_scatter | solution.py:58
  120.0 41.5 %collective-permute-start = (bf16[128,4096]{1,0:T(8,128)(2,1)S(1)}, bf16[128,4096]{1,0:T(8,128)(2,1)S(1)}, u32[]{:S(2)}, u32[]{:S(2)}) collective-permute-start(bf16[128,4096]{1,0:T(8,128)(2,1)S(1)} %reshape.90), channel_id=1, source_target_pairs={{0,32},{32,64},{64,96},{96,0},{1,33},{33,65},{65,97},{97,1},{2,34}... | collective-permute-start | bytes 3145736 | tf_op jit(solution)/shard_map/ppermute | solution.py:19
  120.1 42.2 %collective-permute-start.1 = (bf16[128,4096]{1,0:T(8,128)(2,1)S(1)}, bf16[128,4096]{1,0:T(8,128)(2,1)S(1)}, u32[]{:S(2)}, u32[]{:S(2)}) collective-permute-start(bf16[128,4096]{1,0:T(8,128)(2,1)S(1)} %reshape.90), channel_id=1, source_target_pairs={{0,96},{32,0},{64,32},{96,64},{1,97},{33,1},{65,33},{97,65},{2,98}... | collective-permute-start | bytes 3145736 | tf_op jit(solution)/shard_map/ppermute | solution.py:24
  161.5 25.4 %collective-permute-start.2 = (bf16[128,4096]{1,0:T(8,128)(2,1)S(1)}, bf16[128,4096]{1,0:T(8,128)(2,1)S(1)}, u32[]{:S(2)}, u32[]{:S(2)}) collective-permute-start(bf16[128,4096]{1,0:T(8,128)(2,1)S(1)} %collective-permute-done), channel_id=1, source_target_pairs={{0,32},{32,64},{64,96},{96,0},{1,33},{33,65},{65,97},{97,1},{2,34}... | collective-permute-start | bytes 3145736 | tf_op jit(solution)/shard_map/ppermute | solution.py:19
  201.2 237.2 %reduce-scatter.11.cloned.1.call-start = ((), (), s32[]{:S(2)}) async-start(), calls=%async_computation.15 | async-start | bytes 5242880 | tf_op jit(solution)/shard_map/reduce_scatter | solution.py:58
  230.0 39.0 %collective-permute-start.9 = (bf16[128,4096]{1,0:T(8,128)(2,1)S(1)}, bf16[128,4096]{1,0:T(8,128)(2,1)S(1)}, u32[]{:S(2)}, u32[]{:S(2)}) collective-permute-start(bf16[128,4096]{1,0:T(8,128)(2,1)S(1)} %reshape.100), channel_id=1, source_target_pairs={{0,32},{32,64},{64,96},{96,0},{1,33},{33,65},{65,97},{97,1},{2,34}... | collective-permute-start | bytes 3145736 | tf_op jit(solution)/shard_map/ppermute | solution.py:19
  230.1 39.7 %collective-permute-start.10 = (bf16[128,4096]{1,0:T(8,128)(2,1)S(1)}, bf16[128,4096]{1,0:T(8,128)(2,1)S(1)}, u32[]{:S(2)}, u32[]{:S(2)}) collective-permute-start(bf16[128,4096]{1,0:T(8,128)(2,1)S(1)} %reshape.100), channel_id=1, source_target_pairs={{0,96},{32,0},{64,32},{96,64},{1,97},{33,1},{65,33},{97,65},{2,98}... | collective-permute-start | bytes 3145736 | tf_op jit(solution)/shard_map/ppermute | solution.py:24
  269.0 25.4 %collective-permute-start.11 = (bf16[128,4096]{1,0:T(8,128)(2,1)S(1)}, bf16[128,4096]{1,0:T(8,128)(2,1)S(1)}, u32[]{:S(2)}, u32[]{:S(2)}) collective-permute-start(bf16[128,4096]{1,0:T(8,128)(2,1)S(1)} %collective-permute-done.9), channel_id=1, source_target_pairs={{0,32},{32,64},{64,96},{96,0},{1,33},{33,65},{65,97},{97,1},{2,34}... | collective-permute-start | bytes 3145736 | tf_op jit(solution)/shard_map/ppermute | solution.py:19
  269.5 25.0 %copy-start.10 = (f32[2,512,384]{2,1,0:T(8,128)S(1)}, f32[2,512,384]{2,1,0:T(8,128)}, u32[]{:S(2)}) copy-start(f32[2,512,384]{2,1,0:T(8,128)} %copy-done.9) | copy-start | bytes 4718596
  294.4 4.7 slice-start
  294.5 4.6 slice-start.1
  294.5 4.6 slice-start.2
  304.1 156.2 %reduce-scatter.9.cloned.1.call-start = ((), (), s32[]{:S(2)}) async-start(), calls=%async_computation.14 | async-start | bytes 5242880 | tf_op jit(solution)/shard_map/reduce_scatter | solution.py:58
  331.7 40.1 %collective-permute-start.6 = (bf16[128,4096]{1,0:T(8,128)(2,1)S(1)}, bf16[128,4096]{1,0:T(8,128)(2,1)S(1)}, u32[]{:S(2)}, u32[]{:S(2)}) collective-permute-start(bf16[128,4096]{1,0:T(8,128)(2,1)S(1)} %reshape.97), channel_id=1, source_target_pairs={{0,32},{32,64},{64,96},{96,0},{1,33},{33,65},{65,97},{97,1},{2,34}... | collective-permute-start | bytes 3145736 | tf_op jit(solution)/shard_map/ppermute | solution.py:19
  331.8 40.8 %collective-permute-start.7 = (bf16[128,4096]{1,0:T(8,128)(2,1)S(1)}, bf16[128,4096]{1,0:T(8,128)(2,1)S(1)}, u32[]{:S(2)}, u32[]{:S(2)}) collective-permute-start(bf16[128,4096]{1,0:T(8,128)(2,1)S(1)} %reshape.97), channel_id=1, source_target_pairs={{0,96},{32,0},{64,32},{96,64},{1,97},{33,1},{65,33},{97,65},{2,98}... | collective-permute-start | bytes 3145736 | tf_op jit(solution)/shard_map/ppermute | solution.py:24
  371.8 25.4 %collective-permute-start.8 = (bf16[128,4096]{1,0:T(8,128)(2,1)S(1)}, bf16[128,4096]{1,0:T(8,128)(2,1)S(1)}, u32[]{:S(2)}, u32[]{:S(2)}) collective-permute-start(bf16[128,4096]{1,0:T(8,128)(2,1)S(1)} %collective-permute-done.6), channel_id=1, source_target_pairs={{0,32},{32,64},{64,96},{96,0},{1,33},{33,65},{65,97},{97,1},{2,34}... | collective-permute-start | bytes 3145736 | tf_op jit(solution)/shard_map/ppermute | solution.py:19
  372.3 25.0 %copy-start.8 = (f32[2,512,384]{2,1,0:T(8,128)S(1)}, f32[2,512,384]{2,1,0:T(8,128)}, u32[]{:S(2)}) copy-start(f32[2,512,384]{2,1,0:T(8,128)} %copy-done.7) | copy-start | bytes 4718596
  372.6 29.3 %slice-start.3 = ((s8[9437184]{0:T(1024)(128)(4,1)}), s8[4194304]{0:T(1024)(128)(4,1)S(1)}, s32[]{:S(2)}) async-start(s8[9437184]{0:T(1024)(128)(4,1)} %bitcast.160), calls=%async_computation.19 | async-start | bytes 8388608
  397.4 4.6 slice-start.4
  397.4 4.6 slice-start.5
  409.2 25.3 %all-to-all-start.3 = ((bf16[32,4,4096]{2,1,0:T(4,128)(2,1)}), bf16[32,4,4096]{2,1,0:T(4,128)(2,1)S(1)}, u32[]{:S(2)}, u32[]{:S(2)}) async-start(bf16[32,4,4096]{2,1,0:T(4,128)(2,1)} %reshape.95), calls=%async_computation.5 | async-start | bytes 2097152 | tf_op jit(solution)/shard_map/all_to_all | solution.py:62
  434.5 20.9 %all-to-all-start.1 = ((bf16[32,4,4096]{2,1,0:T(4,128)(2,1)}), bf16[32,4,4096]{2,1,0:T(4,128)(2,1)S(1)}, u32[]{:S(2)}, u32[]{:S(2)}) async-start(bf16[32,4,4096]{2,1,0:T(4,128)(2,1)} %reshape.91), calls=%async_computation.2 | async-start | bytes 2097152 | tf_op jit(solution)/shard_map/all_to_all | solution.py:62
  456.4 20.9 %all-to-all-start.7 = ((bf16[32,4,4096]{2,1,0:T(4,128)(2,1)}), bf16[32,4,4096]{2,1,0:T(4,128)(2,1)S(1)}, u32[]{:S(2)}, u32[]{:S(2)}) async-start(bf16[32,4,4096]{2,1,0:T(4,128)(2,1)} %reshape.101), calls=%async_computation.11 | async-start | bytes 2097152 | tf_op jit(solution)/shard_map/all_to_all | solution.py:62
  477.2 21.4 %all-to-all-start.5 = ((bf16[32,4,4096]{2,1,0:T(4,128)(2,1)}), bf16[32,4,4096]{2,1,0:T(4,128)(2,1)}, u32[]{:S(2)}, u32[]{:S(2)}) async-start(bf16[32,4,4096]{2,1,0:T(4,128)(2,1)} %reshape.98), calls=%async_computation.8 | async-start | bytes 2097152 | tf_op jit(solution)/shard_map/all_to_all | solution.py:62
  481.7 3.2 copy-start.4
  482.6 19.9 %copy-start.1 = (bf16[128,4096]{1,0:T(8,128)(2,1)S(1)}, bf16[128,4096]{1,0:T(8,128)(2,1)}, u32[]{:S(2)}) copy-start(bf16[128,4096]{1,0:T(8,128)(2,1)} %param.5) | copy-start | bytes 3145732
  (5 other events, 5.7 us)
Sparse Core Ops, SparseCore 0:
  96.8 58.1 reduce-scatter.6
  201.4 58.5 reduce-scatter.4
  304.2 59.6 reduce-scatter.10
  407.1 46.3 reduce-scatter.8
